TPU v7x, 256 devices: a whole 4x4x8 slice. The times are simulated.
256 devices in a mesh: expert: 32 (over x, z), tensor: 8 (over y, core).
Axes of the slice: x: 4, y: 4, z: 8, core: 2. Of those that a mesh axis runs over, the one named last changes fastest.
Arguments:
- attn_vals: bfloat16 [2048, 4096], P('expert', 'tensor'), may hold values from -6 to 6
- residual: bfloat16 [2048, 4096], P('expert', 'tensor'), may hold values from -6 to 6
- out_weight: bfloat16 [4096, 4096], P('tensor'), may hold values from -0.09375 to 0.09375
- norm_gain: float32 [4096], P('tensor'), may hold values from 0.5 to 1.5
- router_weight: float32 [4096, 8], P('tensor'), may hold values from -0.09375 to 0.09375
- routes: int32 [2048, 2], P('expert'), may hold values from 0 to 7, all different within a row; in each aligned block of 64 rows (0 to 63, 64 to 127, ...) at most 32 rows name the same one
- w_gate: bfloat16 [32, 4096, 2048], P('expert', None, 'tensor'), may hold values from -0.09375 to 0.09375
- w_up: bfloat16 [32, 4096, 2048], P('expert', None, 'tensor'), may hold values from -0.09375 to 0.09375
- w_down: bfloat16 [32, 2048, 4096], P('expert', 'tensor'), may hold values from -0.0625 to 0.0625
- slab_of: int32 [32], replicated, may hold values from 0 to 31, each once
- final_gain: float32 [4096], P('tensor'), may hold values from 0.5 to 1.5
- row_order: int32 [2048], replicated, may hold values from 0 to 2047, each once
Outputs:
- stream_out: bfloat16 [2048, 4096], P('expert', 'tensor')
- normed_out: bfloat16 [2048, 4096], P('expert', 'tensor')
Inputs may be any that keep to these rules, and one draw needn't show every extreme that they name: `routes`: the two experts of a row differ. In each aligned block of 64 rows (the rows of one device) no expert is named by more than 32 rows, and some block names one expert exactly 32 times. `slab_of`: A permutation. `row_order`: A permutation.
All inputs are finite; a program needn't handle non-finite values.
Results may differ from a plain program's by a relative error of at most 0.017.
Values may be sent and summed in bfloat16 or wider, within the bound.
No kernel may reach another device: no remote copies, remote signals or barrier semaphores. Data moves between devices by JAX's collectives and lax.ppermute only.
A program may use at most 128 MiB of HBM per device.

v0:
```python
import jax
import jax.numpy as jnp
from jax import lax
from jax.sharding import PartitionSpec as P

D = 4096
MOST = 32
EPS = 1e-05


def finish_slots(gate_val, up_val, down_weight):
    active = (jax.nn.silu(gate_val) * up_val).astype(jnp.bfloat16)
    partial_out = jnp.einsum("gmf,fd->gmd", active, down_weight, preferred_element_type=jnp.float32)
    summed = lax.psum_scatter(
        partial_out.astype(jnp.bfloat16), "tensor", scatter_dimension=2, tiled=True
    )
    return lax.all_to_all(summed, "expert", split_axis=0, concat_axis=0, tiled=True)


def final_norm(stream, final_gain):
    stream_f = stream.astype(jnp.float32)
    square_total = lax.psum(jnp.sum(stream_f * stream_f, axis=1), "tensor")
    factor = lax.rsqrt(square_total / D + EPS)
    return (stream_f * factor[:, None] * final_gain).astype(jnp.bfloat16)


def on_device(
    attn_vals,
    residual,
    out_weight,
    norm_gain,
    router_weight,
    routes,
    w_gate,
    w_up,
    w_down,
    slab_of,
    final_gain,
    row_order,
):
    groups = lax.axis_size("expert")
    row_count = attn_vals.shape[0]
    expert_count = router_weight.shape[1]
    slab_count = groups // expert_count
    partial_proj = jnp.dot(attn_vals, out_weight, preferred_element_type=jnp.float32)
    project = lax.psum_scatter(
        partial_proj.astype(jnp.bfloat16), "tensor", scatter_dimension=1, tiled=True
    ).astype(jnp.float32)
    stream_in = (residual.astype(jnp.float32) + project).astype(jnp.bfloat16)
    hidden_f = stream_in.astype(jnp.float32)
    scaled = hidden_f * norm_gain
    square_sum, logit_part = lax.psum(
        (
            jnp.sum(hidden_f * hidden_f, axis=1),
            jnp.dot(scaled, router_weight, precision=lax.Precision.HIGHEST),
        ),
        "tensor",
    )
    inverse_rms = lax.rsqrt(square_sum / D + EPS)
    normed_in = (scaled * inverse_rms[:, None]).astype(jnp.bfloat16)
    logits = logit_part * inverse_rms[:, None]
    expert_ids = jnp.arange(expert_count, dtype=jnp.int32)
    route_hot = (routes[:, :, None] == expert_ids[None, None, :]).astype(jnp.int32)
    chosen = jnp.sum(route_hot.astype(jnp.float32) * logits[:, None, :], axis=2)
    leading = jax.nn.sigmoid(chosen[:, 0] - chosen[:, 1])
    mixing = jnp.stack([leading, 1.0 - leading], axis=1)
    route_hits = jnp.sum(route_hot, axis=1)
    before_count = jnp.cumsum(route_hits, axis=0) - route_hits
    slot_ids = jnp.sum(route_hot * before_count[:, None, :], axis=2)
    slot_hot = (slot_ids[:, :, None] == jnp.arange(MOST, dtype=jnp.int32)[None, None, :]).astype(
        jnp.float32
    )
    placing = jnp.einsum("rke,rks->esr", route_hot.astype(jnp.float32), slot_hot).astype(
        jnp.bfloat16
    )
    target_expert = slab_of // slab_count
    send_map = jnp.take(placing, target_expert, axis=0)
    full_rows = lax.all_gather(normed_in, "tensor", axis=1, tiled=True)
    outgoing = jnp.einsum(
        "gsr,rd->gsd", send_map, full_rows, preferred_element_type=jnp.float32
    ).astype(jnp.bfloat16)
    arrived = lax.all_to_all(outgoing, "expert", split_axis=0, concat_axis=0, tiled=True)
    gate_val = jnp.einsum("gmd,df->gmf", arrived, w_gate[0], preferred_element_type=jnp.float32)
    up_val = jnp.einsum("gmd,df->gmf", arrived, w_up[0], preferred_element_type=jnp.float32)
    returned = finish_slots(gate_val, up_val, w_down[0])
    group_ids = jnp.arange(groups, dtype=jnp.int32)
    holder_hot = (slab_of[None, :] == group_ids[:, None]).astype(jnp.int32)
    holders = jnp.sum(holder_hot * group_ids[None, :], axis=1).reshape(expert_count, slab_count)
    row_holders = jnp.take(holders, routes, axis=0)
    flat_index = row_holders * MOST + slot_ids[:, :, None]
    flat_back = returned.reshape(groups * MOST, returned.shape[2])
    fetched = jnp.take(flat_back, flat_index.reshape(-1), axis=0).reshape(
        row_count, 2, slab_count, returned.shape[2]
    )
    expert_out = jnp.sum(fetched.astype(jnp.float32), axis=2)
    blended = jnp.sum(mixing[:, :, None] * expert_out, axis=1)
    stream = (hidden_f + blended).astype(jnp.bfloat16)
    positions = lax.axis_index("expert") * row_count + jnp.arange(row_count, dtype=jnp.int32)
    matches = (row_order[None, :] == positions[:, None]).astype(jnp.int32)
    source = jnp.sum(matches * jnp.arange(row_order.shape[0], dtype=jnp.int32)[None, :], axis=1)
    normed = final_norm(stream, final_gain)
    all_stream, all_normed = (
        lax.all_gather(stream, "expert", axis=0, tiled=True),
        lax.all_gather(normed, "expert", axis=0, tiled=True),
    )
    return (jnp.take(all_stream, source, axis=0), jnp.take(all_normed, source, axis=0))


def solution(mesh):
    return jax.shard_map(
        on_device,
        mesh=mesh,
        in_specs=(
            P("expert", "tensor"),
            P("expert", "tensor"),
            P("tensor", None),
            P("tensor"),
            P("tensor", None),
            P("expert", None),
            P("expert", None, "tensor"),
            P("expert", None, "tensor"),
            P("expert", "tensor", None),
            P(),
            P("tensor"),
            P(),
        ),
        out_specs=(P("expert", "tensor"), P("expert", "tensor")),
        check_vma=False,
    )
```

profile of v0, /device:TPU:8, one launch (start us, length us, event | category | flops | bytes accessed | tf_op | source)
XLA Modules:
  0.0 564.1 jit_solution(10908743373798955551)
XLA Ops:
  7.3 4.0 convolution_convert_fusion.2
  11.3 0.1 copy.71
  11.4 0.2 convert_reduce_fusion.1
  11.6 0.1 reduce_window_sum.11
  11.7 1.2 select_reduce_fusion.1
  13.0 0.4 fusion.13
  13.4 0.1 copy.80
  13.6 0.6 gather_fusion.1
  14.2 31.1 %reduce-scatter.3.cloned.1.call-done = bf16[64,512]{1,0:T(8,128)(2,1)} async-done(((bf16[64,4096]{1,0:T(8,128)(2,1)}), bf16[64,512]{1,0:T(8,128)(2,1)}) %reduce-scatter.3.cloned.1.call-update) | async-done | bytes 65552 | tf_op jit(solution)/shard_map/reduce_scatter | solution.py:46
  45.3 1.0 fusion.29
  46.3 0.2 fusion.24
  46.4 13.4 %all-reduce = (f32[64]{0:T(128)S(1)}, f32[64,8]{0,1:T(8,128)S(1)}) all-reduce(f32[64]{0:T(128)S(1)} %get-tuple-element.13, f32[64,8]{0,1:T(8,128)S(1)} %fusion.24), channel_id=1, replica_groups=mesh['expert'=32,'tensor'=8] {'tensor'}, use_global_device_ids=true, to_apply=%region_3.0 | all-reduce | flops 576 | bytes 4608 | tf_op jit(solution)/shard_map/psum | solution.py:52
  59.9 0.1 fusion.25
  60.0 13.6 %all_gather.9 = bf16[64,4096]{1,0:T(8,128)(2,1)S(1)} all-gather(bf16[64,512]{1,0:T(8,128)(2,1)S(1)} %fusion.25), channel_id=1, replica_groups=mesh['expert'=32,'tensor'=8] {'tensor'}, dimensions={1}, use_global_device_ids=true | all-gather | bytes 589824 | tf_op jit(solution)/shard_map/all_gather | solution.py:78
  73.5 2.4 convolution_convert_fusion.1
  75.9 195.8 %all_to_all.10 = bf16[32,32,4096]{2,1,0:T(8,128)(2,1)S(1)} all-to-all(bf16[32,32,4096]{2,1,0:T(8,128)(2,1)S(1)} %convolution_convert_fusion.1), channel_id=1, replica_groups=mesh['expert'=32,'tensor'=8] {'expert'}, dimensions={0} | all-to-all | bytes 16777216 | tf_op jit(solution)/shard_map/all_to_all | solution.py:82
  271.7 3.2 copy-done.1
  275.0 2.3 fusion.3
  277.3 16.8 %convolution_convert_fusion = bf16[32,32,4096]{2,1,0:T(8,128)(2,1)} fusion(bf16[1,256,4096]{2,1,0:T(8,128)(2,1)S(1)} %copy-done, bf16[32,32,4096]{2,1,0:T(8,128)(2,1)} %copy-done.1, bf16[1,4096,256]{2,1,0:T(8,128)(2,1)} %param.21, f32[32,32,256]{2,1,0:T(8,128)S(1)} %fusion.3), kind=kOutput, calls=%fused_computation.5 | convolution fusion | flops 4300734464 | bytes 22020096 | tf_op jit(solution)/shard_map/gmf,fd->gmd/dot_general | solution.py:13
  294.2 50.3 %reduce-scatter.5.cloned.1.call-done = bf16[32,32,512]{2,1,0:T(8,128)(2,1)} async-done(((bf16[32,32,4096]{2,1,0:T(8,128)(2,1)}), bf16[32,32,512]{2,1,0:T(8,128)(2,1)}) %reduce-scatter.5.cloned.1.call-update) | async-done | bytes 1048592 | tf_op jit(solution)/shard_map/reduce_scatter | solution.py:14
  344.5 10.0 %all-to-all-start.1 = ((bf16[32,32,512]{2,1,0:T(8,128)(2,1)}), bf16[32,32,512]{2,1,0:T(8,128)(2,1)S(1)}, u32[]{:S(2)}, u32[]{:S(2)}) async-start(bf16[32,32,512]{2,1,0:T(8,128)(2,1)} %reduce-scatter.5.cloned.1.call-done), calls=%async_computation.3 | async-start | bytes 2097152 | tf_op jit(solution)/shard_map/all_to_all | solution.py:17
  354.6 0.1 copy.76
  354.7 0.1 reshape.132
  354.9 0.1 select_reduce_fusion.2
  355.0 0.1 reshape.112
  355.1 0.6 gather_fusion
  355.8 0.1 copy.77
  355.9 0.1 copy.81
  356.0 0.1 add.120
  356.1 0.1 copy.79
  356.3 0.1 copy.72
  356.4 0.2 fusion.34
  356.9 0.1 copy.75
  357.0 26.1 %all-to-all-done.1 = bf16[32,32,512]{2,1,0:T(8,128)(2,1)S(1)} async-done(((bf16[32,32,512]{2,1,0:T(8,128)(2,1)}), bf16[32,32,512]{2,1,0:T(8,128)(2,1)S(1)}, u32[]{:S(2)}, u32[]{:S(2)}) %all-to-all-start.1) | async-done | bytes 1048608 | tf_op jit(solution)/shard_map/all_to_all | solution.py:17
  383.2 2.6 gather_fusion.2
  385.8 1.2 gather.20
  386.9 0.9 convert_reduce_fusion
  387.9 0.4 multiply_reduce_fusion
  388.3 0.1 fusion.26
  388.4 11.3 %psum.23 = f32[64]{0:T(128)S(1)} all-reduce(f32[64]{0:T(128)S(1)} %get-tuple-element.5), channel_id=1, replica_groups=mesh['expert'=32,'tensor'=8] {'tensor'}, use_global_device_ids=true, to_apply=%region_14.16 | all-reduce | flops 64 | bytes 512 | tf_op jit(solution)/shard_map/psum | solution.py:22
  399.7 0.7 fusion.28
  400.5 0.5 all-gather.3.cloned.1.call-update
  401.0 0.2 select_reduce_fusion
  401.3 74.9 %all-gather.5.cloned.1.call-done = bf16[2048,512]{1,0:T(8,128)(2,1)} async-done(((bf16[64,512]{1,0:T(8,128)(2,1)}), bf16[2048,512]{1,0:T(8,128)(2,1)}) %all-gather.5.cloned.1.call-update) | async-done | bytes 2097168 | tf_op jit(solution)/shard_map/all_gather | solution.py:104
  476.1 2.6 gather_fusion.4
  478.7 75.6 %all-gather.3.cloned.1.call-done = bf16[2048,512]{1,0:T(8,128)(2,1)} async-done(((bf16[64,512]{1,0:T(8,128)(2,1)}), bf16[2048,512]{1,0:T(8,128)(2,1)}) %all-gather.3.cloned.1.call-update) | async-done | bytes 2097168 | tf_op jit(solution)/shard_map/all_gather | solution.py:103
  554.3 2.6 gather_fusion.3
  556.9 0.7 broadcast_select_fusion
  (50 shorter events, 0.7 us)
Async XLA Ops:
  7.2 270.1 %copy-start = (bf16[1,256,4096]{2,1,0:T(8,128)(2,1)S(1)}, bf16[1,256,4096]{2,1,0:T(8,128)(2,1)}, u32[]{:S(2)}) copy-start(bf16[1,256,4096]{2,1,0:T(8,128)(2,1)} %param.22) | copy-start | bytes 6291460
  7.2 4.2 copy-start.7
  7.2 6.4 %copy-start.10 = (s32[32]{0:T(128)S(1)}, s32[32]{0:T(128)}, u32[]{:S(2)}) copy-start(s32[32]{0:T(128)} %param.23) | copy-start | bytes 388
  7.2 38.1 %copy-start.3 = (bf16[64,512]{1,0:T(8,128)(2,1)S(1)}, bf16[64,512]{1,0:T(8,128)(2,1)}, u32[]{:S(2)}) copy-start(bf16[64,512]{1,0:T(8,128)(2,1)} %param.15) | copy-start | bytes 196612
  7.2 39.0 %copy-start.5 = (f32[512]{0:T(512)S(1)}, f32[512]{0:T(512)}, u32[]{:S(2)}) copy-start(f32[512]{0:T(512)} %param.17) | copy-start | bytes 6148
  7.2 39.0 %copy-start.4 = (f32[512,8]{0,1:T(8,128)S(1)}, f32[512,8]{0,1:T(8,128)}, u32[]{:S(2)}) copy-start(f32[512,8]{0,1:T(8,128)} %param.18) | copy-start | bytes 49156
  7.2 38.0 %reduce-scatter.3.cloned.1.call-start = ((), (), s32[]{:S(2)}) async-start(), calls=%async_computation.4 | async-start | bytes 589824 | tf_op jit(solution)/shard_map/reduce_scatter | solution.py:46
  11.3 333.2 %reduce-scatter.5.cloned.1.call-start = ((), (), s32[]{:S(2)}) async-start(), calls=%async_computation.5 | async-start | bytes 9437184 | tf_op jit(solution)/shard_map/reduce_scatter | solution.py:14
  75.9 199.0 %copy-start.9 = (bf16[1,4096,256]{2,1,0:T(8,128)(2,1)S(1)}, bf16[1,4096,256]{2,1,0:T(8,128)(2,1)}, u32[]{:S(2)}) copy-start(bf16[1,4096,256]{2,1,0:T(8,128)(2,1)} %param.20) | copy-start | bytes 6291460
  271.7 3.2 copy-start.1
  344.5 38.7 %all-to-all-start.1 = ((bf16[32,32,512]{2,1,0:T(8,128)(2,1)}), bf16[32,32,512]{2,1,0:T(8,128)(2,1)S(1)}, u32[]{:S(2)}, u32[]{:S(2)}) async-start(bf16[32,32,512]{2,1,0:T(8,128)(2,1)} %reduce-scatter.5.cloned.1.call-done), calls=%async_computation.3 | async-start | bytes 2097152 | tf_op jit(solution)/shard_map/all_to_all | solution.py:17
  354.5 121.6 %all-gather.5.cloned.1.call-start = ((), (), s32[]{:S(2)}) async-start(), calls=%async_computation.7 | async-start | bytes 2162688 | tf_op jit(solution)/shard_map/all_gather | solution.py:104
  355.1 44.6 %copy-start.8 = (f32[512]{0:T(512)S(1)}, f32[512]{0:T(512)}, u32[]{:S(2)}) copy-start(f32[512]{0:T(512)} %param.24) | copy-start | bytes 6148
  355.8 45.3 %copy-start.6 = (s32[2048]{0:T(1024)S(1)}, s32[2048]{0:T(1024)}, u32[]{:S(2)}) copy-start(s32[2048]{0:T(1024)} %param.25) | copy-start | bytes 24580
  388.4 12.1 %copy-start.2 = (bf16[64,512]{1,0:T(8,128)(2,1)}, bf16[64,512]{1,0:T(8,128)(2,1)S(1)}, u32[]{:S(2)}) copy-start(bf16[64,512]{1,0:T(8,128)(2,1)S(1)} %get-tuple-element.6) | copy-start | bytes 196612
  400.4 153.9 %all-gather.3.cloned.1.call-start = ((), (), s32[]{:S(2)}) async-start(), calls=%async_computation.6 | async-start | bytes 2162688 | tf_op jit(solution)/shard_map/all_gather | solution.py:103
Sparse Core Ops, SparseCore 0:
  11.4 33.8 reduce-scatter.2
  294.3 50.1 reduce-scatter.4
  400.5 75.5 all-gather.4
  479.2 75.1 all-gather.2
where the time goes:
time: 565 us; the launch traced here: 564 us
  waiting for transfers between devices  259 us (46%)
  blocking collectives  234 us (41%)
  matrix products  26.2 us (5%)
  local copies, waits for them, and re-layouts  14.9 us (3%)
  between operations  14.1 us (2%)
  starting transfers between devices  10.2 us (2%)
  other arithmetic  6.14 us (1%)
    all_to_all x1, blocking collectives, on_device(): lax.all_to_all(outgoing, 'expert', split_axis=0, concat_axis=0, tiled=True)  196 us
    all_gather x1, waiting for transfers between devices, on_device(): lax.all_gather(stream, 'expert', axis=0, tiled=True)  75.6 us
    all_gather x1, waiting for transfers between devices, on_device(): lax.all_gather(normed, 'expert', axis=0, tiled=True)  74.9 us
    reduce_scatter x1, waiting for transfers between devices, finish_slots(): lax.psum_scatter(partial_out.astype(jnp.bfloat16), 'tensor', scatter_dime...  50.3 us
    reduce_scatter x1, waiting for transfers between devices, on_device(): lax.psum_scatter(partial_proj.astype(jnp.bfloat16), 'tensor', scatter_dim...  31.1 us
    all_to_all x1, waiting for transfers between devices, finish_slots(): lax.all_to_all(summed, 'expert', split_axis=0, concat_axis=0, tiled=True)  26.1 us
    dot_general x1, matrix products, finish_slots(): jnp.einsum('gmf,fd->gmd', active, down_weight, preferred_element_type=jnp...  16.8 us
    all_gather x1, blocking collectives, on_device(): full_rows = lax.all_gather(normed_in, 'tensor', axis=1, tiled=True)  13.6 us
  transfers between devices with their start and end apart: 5, of which 5 were waited for; matrix products, arithmetic and copies ran while one was open for 1% of the time, Pallas kernels for 0%

commit v1 on v0

--- a/solution.py
+++ b/solution.py
@@ -101,7 +101,9 @@
     normed = final_norm(stream, final_gain)
     all_stream, all_normed = (
         lax.all_gather(stream, "expert", axis=0, tiled=True),
-        lax.all_gather(normed, "expert", axis=0, tiled=True),
+        jnp.concatenate(
+            lax.all_to_all(jnp.stack([normed] * lax.axis_size("expert")), "expert", 0, 0), axis=0
+        ),
     )
     return (jnp.take(all_stream, source, axis=0), jnp.take(all_normed, source, axis=0))
 

time: 565 us -> 504 us (0.89)
  waiting for transfers between devices: 259 us -> 191 us
  starting transfers between devices: 10.2 us -> 16 us
    all_gather x1 -> x0, waiting for transfers between devices: 74.9 us -> none  [on_device(): lax.all_gather(normed, 'expert', axis=0, tiled=True)]
    all_to_all x0 -> x1, waiting for transfers between devices: none -> 51.4 us  [on_device(): lax.all_to_all(jnp.stack([normed] * lax.axis_size('expert')), 'expert', 0...]
    all_gather x1, waiting for transfers between devices: 75.6 us -> 31.2 us  [on_device(): lax.all_gather(stream, 'expert', axis=0, tiled=True)]
    all_to_all x0 -> x1, starting transfers between devices: none -> 5.86 us  [on_device(): lax.all_to_all(jnp.stack([normed] * lax.axis_size('expert')), 'expert', 0...]
  transfers between devices with their start and end apart: 5 -> 5, of which waited for: 5 -> 5; matrix products, arithmetic and copies ran while one was open for 1% -> 2% of each run, Pallas kernels for 0% -> 0%
where the time goes in v1:
time: 504 us; the launch traced here: 503 us
  blocking collectives  234 us (46%)
  waiting for transfers between devices  191 us (38%)
  matrix products  26.2 us (5%)
  local copies, waits for them, and re-layouts  16.5 us (3%)
  starting transfers between devices  16 us (3%)
  between operations  14.1 us (3%)
  other arithmetic  5.51 us (1%)
    all_to_all x1, blocking collectives, on_device(): lax.all_to_all(outgoing, 'expert', split_axis=0, concat_axis=0, tiled=True)  196 us
    all_to_all x1, waiting for transfers between devices, on_device(): lax.all_to_all(jnp.stack([normed] * lax.axis_size('expert')), 'expert', 0...  51.4 us
    reduce_scatter x1, waiting for transfers between devices, finish_slots(): lax.psum_scatter(partial_out.astype(jnp.bfloat16), 'tensor', scatter_dime...  50.3 us
    all_gather x1, waiting for transfers between devices, on_device(): lax.all_gather(stream, 'expert', axis=0, tiled=True)  31.2 us
    reduce_scatter x1, waiting for transfers between devices, on_device(): lax.psum_scatter(partial_proj.astype(jnp.bfloat16), 'tensor', scatter_dim...  31.1 us
    all_to_all x1, waiting for transfers between devices, finish_slots(): lax.all_to_all(summed, 'expert', split_axis=0, concat_axis=0, tiled=True)  26.2 us
    dot_general x1, matrix products, finish_slots(): jnp.einsum('gmf,fd->gmd', active, down_weight, preferred_element_type=jnp...  16.8 us
    all_gather x1, blocking collectives, on_device(): full_rows = lax.all_gather(normed_in, 'tensor', axis=1, tiled=True)  13.6 us
  transfers between devices with their start and end apart: 5, of which 5 were waited for; matrix products, arithmetic and copies ran while one was open for 2% of the time, Pallas kernels for 0%

profile of v1, /device:TPU:8, one launch (start us, length us, event | category | flops | bytes accessed | tf_op | source)
XLA Modules:
  0.0 503.3 jit_solution(18104267679460051192)
XLA Ops:
  7.3 4.0 convolution_convert_fusion.2
  11.3 0.1 copy.71
  11.4 0.2 convert_reduce_fusion.1
  11.6 0.1 reduce_window_sum.11
  11.7 1.2 select_reduce_fusion.1
  13.0 0.4 fusion.13
  13.4 0.1 copy.80
  13.6 0.6 gather_fusion.1
  14.2 31.1 %reduce-scatter.3.cloned.1.call-done = bf16[64,512]{1,0:T(8,128)(2,1)} async-done(((bf16[64,4096]{1,0:T(8,128)(2,1)}), bf16[64,512]{1,0:T(8,128)(2,1)}) %reduce-scatter.3.cloned.1.call-update) | async-done | bytes 65552 | tf_op jit(solution)/shard_map/reduce_scatter | solution.py:46
  45.3 1.0 fusion.29
  46.3 0.2 fusion.24
  46.4 13.4 %all-reduce = (f32[64]{0:T(128)S(1)}, f32[64,8]{0,1:T(8,128)S(1)}) all-reduce(f32[64]{0:T(128)S(1)} %get-tuple-element.13, f32[64,8]{0,1:T(8,128)S(1)} %fusion.24), channel_id=1, replica_groups=mesh['expert'=32,'tensor'=8] {'tensor'}, use_global_device_ids=true, to_apply=%region_3.0 | all-reduce | flops 576 | bytes 4608 | tf_op jit(solution)/shard_map/psum | solution.py:52
  60.0 13.6 %all_gather.6 = bf16[64,4096]{1,0:T(8,128)(2,1)S(1)} all-gather(bf16[64,512]{1,0:T(8,128)(2,1)S(1)} %fusion.25), channel_id=1, replica_groups=mesh['expert'=32,'tensor'=8] {'tensor'}, dimensions={1}, use_global_device_ids=true | all-gather | bytes 589824 | tf_op jit(solution)/shard_map/all_gather | solution.py:78
  73.5 2.4 convolution_convert_fusion.1
  75.9 195.8 %all_to_all.15 = bf16[32,32,4096]{2,1,0:T(8,128)(2,1)S(1)} all-to-all(bf16[32,32,4096]{2,1,0:T(8,128)(2,1)S(1)} %convolution_convert_fusion.1), channel_id=1, replica_groups=mesh['expert'=32,'tensor'=8] {'expert'}, dimensions={0} | all-to-all | bytes 16777216 | tf_op jit(solution)/shard_map/all_to_all | solution.py:82
  271.7 3.2 copy-done.1
  275.0 2.3 fusion.3
  277.3 16.8 %convolution_convert_fusion = bf16[32,32,4096]{2,1,0:T(8,128)(2,1)} fusion(bf16[1,256,4096]{2,1,0:T(8,128)(2,1)S(1)} %copy-done, bf16[32,32,4096]{2,1,0:T(8,128)(2,1)} %copy-done.1, bf16[1,4096,256]{2,1,0:T(8,128)(2,1)} %param.21, f32[32,32,256]{2,1,0:T(8,128)S(1)} %fusion.3), kind=kOutput, calls=%fused_computation.5 | convolution fusion | flops 4300734464 | bytes 22020096 | tf_op jit(solution)/shard_map/gmf,fd->gmd/dot_general | solution.py:13
  294.2 50.3 %reduce-scatter.5.cloned.1.call-done = bf16[32,32,512]{2,1,0:T(8,128)(2,1)} async-done(((bf16[32,32,4096]{2,1,0:T(8,128)(2,1)}), bf16[32,32,512]{2,1,0:T(8,128)(2,1)}) %reduce-scatter.5.cloned.1.call-update) | async-done | bytes 1048592 | tf_op jit(solution)/shard_map/reduce_scatter | solution.py:14
  344.5 10.0 %all-to-all-start.1 = ((bf16[32,32,512]{2,1,0:T(8,128)(2,1)}), bf16[32,32,512]{2,1,0:T(8,128)(2,1)S(1)}, u32[]{:S(2)}, u32[]{:S(2)}) async-start(bf16[32,32,512]{2,1,0:T(8,128)(2,1)} %reduce-scatter.5.cloned.1.call-done), calls=%async_computation.3 | async-start | bytes 2097152 | tf_op jit(solution)/shard_map/all_to_all | solution.py:17
  354.6 0.1 copy.76
  354.7 0.1 reshape.138
  354.8 0.1 select_reduce_fusion.2
  355.1 0.6 gather_fusion
  355.7 0.1 copy.77
  355.8 0.1 copy.81
  355.9 0.1 add.120
  356.1 0.1 copy.79
  356.3 0.1 copy.72
  356.4 0.2 fusion.34
  356.9 0.1 copy.75
  357.0 26.2 %all-to-all-done.1 = bf16[32,32,512]{2,1,0:T(8,128)(2,1)S(1)} async-done(((bf16[32,32,512]{2,1,0:T(8,128)(2,1)}), bf16[32,32,512]{2,1,0:T(8,128)(2,1)S(1)}, u32[]{:S(2)}, u32[]{:S(2)}) %all-to-all-start.1) | async-done | bytes 1048608 | tf_op jit(solution)/shard_map/all_to_all | solution.py:17
  383.2 2.6 gather_fusion.2
  385.8 1.2 gather.20
  387.0 0.9 convert_reduce_fusion
  387.9 0.4 multiply_reduce_fusion
  388.3 0.1 fusion.26
  388.4 11.3 %psum.23 = f32[64]{0:T(128)S(1)} all-reduce(f32[64]{0:T(128)S(1)} %get-tuple-element.5), channel_id=1, replica_groups=mesh['expert'=32,'tensor'=8] {'tensor'}, use_global_device_ids=true, to_apply=%region_14.16 | all-reduce | flops 64 | bytes 512 | tf_op jit(solution)/shard_map/psum | solution.py:22
  399.7 0.1 fusion.28
  399.8 1.6 stack.5
  401.3 5.9 %all-to-all-start.2 = ((bf16[32,64,512]{2,1,0:T(8,128)(2,1)}), bf16[32,64,512]{2,1,0:T(8,128)(2,1)}, u32[]{:S(2)}, u32[]{:S(2)}) async-start(bf16[32,64,512]{2,1,0:T(8,128)(2,1)} %stack.5), calls=%async_computation.4 | async-start | bytes 4194304 | tf_op jit(solution)/shard_map/all_to_all | solution.py:105
  407.3 0.7 all-gather.2.cloned.1.call-update
  408.0 0.2 select_reduce_fusion
  408.2 51.4 %all-to-all-done.2 = bf16[32,64,512]{2,1,0:T(8,128)(2,1)} async-done(((bf16[32,64,512]{2,1,0:T(8,128)(2,1)}), bf16[32,64,512]{2,1,0:T(8,128)(2,1)}, u32[]{:S(2)}, u32[]{:S(2)}) %all-to-all-start.2) | async-done | bytes 2097184 | tf_op jit(solution)/shard_map/all_to_all | solution.py:105
  459.6 2.6 gather_fusion.4
  462.2 31.2 %all-gather.2.cloned.1.call-done = bf16[2048,512]{1,0:T(8,128)(2,1)} async-done(((bf16[64,512]{1,0:T(8,128)(2,1)}), bf16[2048,512]{1,0:T(8,128)(2,1)}) %all-gather.2.cloned.1.call-update) | async-done | bytes 2097168 | tf_op jit(solution)/shard_map/all_gather | solution.py:103
  493.4 2.6 gather_fusion.3
  496.0 0.7 broadcast_select_fusion
  (50 shorter events, 0.8 us)
Async XLA Ops:
  7.2 270.1 %copy-start = (bf16[1,256,4096]{2,1,0:T(8,128)(2,1)S(1)}, bf16[1,256,4096]{2,1,0:T(8,128)(2,1)}, u32[]{:S(2)}) copy-start(bf16[1,256,4096]{2,1,0:T(8,128)(2,1)} %param.22) | copy-start | bytes 6291460
  7.2 4.2 copy-start.7
  7.2 6.4 %copy-start.10 = (s32[32]{0:T(128)S(1)}, s32[32]{0:T(128)}, u32[]{:S(2)}) copy-start(s32[32]{0:T(128)} %param.23) | copy-start | bytes 388
  7.2 38.1 %copy-start.3 = (bf16[64,512]{1,0:T(8,128)(2,1)S(1)}, bf16[64,512]{1,0:T(8,128)(2,1)}, u32[]{:S(2)}) copy-start(bf16[64,512]{1,0:T(8,128)(2,1)} %param.15) | copy-start | bytes 196612
  7.2 39.0 %copy-start.5 = (f32[512]{0:T(512)S(1)}, f32[512]{0:T(512)}, u32[]{:S(2)}) copy-start(f32[512]{0:T(512)} %param.17) | copy-start | bytes 6148
  7.2 39.0 %copy-start.4 = (f32[512,8]{0,1:T(8,128)S(1)}, f32[512,8]{0,1:T(8,128)}, u32[]{:S(2)}) copy-start(f32[512,8]{0,1:T(8,128)} %param.18) | copy-start | bytes 49156
  7.2 38.0 %reduce-scatter.3.cloned.1.call-start = ((), (), s32[]{:S(2)}) async-start(), calls=%async_computation.5 | async-start | bytes 589824 | tf_op jit(solution)/shard_map/reduce_scatter | solution.py:46
  11.3 333.2 %reduce-scatter.5.cloned.1.call-start = ((), (), s32[]{:S(2)}) async-start(), calls=%async_computation.6 | async-start | bytes 9437184 | tf_op jit(solution)/shard_map/reduce_scatter | solution.py:14
  75.9 199.0 %copy-start.9 = (bf16[1,4096,256]{2,1,0:T(8,128)(2,1)S(1)}, bf16[1,4096,256]{2,1,0:T(8,128)(2,1)}, u32[]{:S(2)}) copy-start(bf16[1,4096,256]{2,1,0:T(8,128)(2,1)} %param.20) | copy-start | bytes 6291460
  271.7 3.2 copy-start.1
  344.5 38.7 %all-to-all-start.1 = ((bf16[32,32,512]{2,1,0:T(8,128)(2,1)}), bf16[32,32,512]{2,1,0:T(8,128)(2,1)S(1)}, u32[]{:S(2)}, u32[]{:S(2)}) async-start(bf16[32,32,512]{2,1,0:T(8,128)(2,1)} %reduce-scatter.5.cloned.1.call-done), calls=%async_computation.3 | async-start | bytes 2097152 | tf_op jit(solution)/shard_map/all_to_all | solution.py:17
  355.1 44.6 %copy-start.8 = (f32[512]{0:T(512)S(1)}, f32[512]{0:T(512)}, u32[]{:S(2)}) copy-start(f32[512]{0:T(512)} %param.24) | copy-start | bytes 6148
  386.9 21.0 %copy-start.6 = (s32[2048]{0:T(1024)S(1)}, s32[2048]{0:T(1024)}, u32[]{:S(2)}) copy-start(s32[2048]{0:T(1024)} %param.25) | copy-start | bytes 24580
  388.4 18.9 %copy-start.2 = (bf16[64,512]{1,0:T(8,128)(2,1)}, bf16[64,512]{1,0:T(8,128)(2,1)S(1)}, u32[]{:S(2)}) copy-start(bf16[64,512]{1,0:T(8,128)(2,1)S(1)} %get-tuple-element.6) | copy-start | bytes 196612
  401.3 58.3 %all-to-all-start.2 = ((bf16[32,64,512]{2,1,0:T(8,128)(2,1)}), bf16[32,64,512]{2,1,0:T(8,128)(2,1)}, u32[]{:S(2)}, u32[]{:S(2)}) async-start(bf16[32,64,512]{2,1,0:T(8,128)(2,1)} %stack.5), calls=%async_computation.4 | async-start | bytes 4194304 | tf_op jit(solution)/shard_map/all_to_all | solution.py:105
  407.2 86.2 %all-gather.2.cloned.1.call-start = ((), (), s32[]{:S(2)}) async-start(), calls=%async_computation.7 | async-start | bytes 2162688 | tf_op jit(solution)/shard_map/all_gather | solution.py:103
Sparse Core Ops, SparseCore 0:
  11.4 33.8 reduce-scatter.2
  294.3 50.1 reduce-scatter.4
  411.2 82.2 all-gather.1
